TPU v7x, 128 devices: a whole 4x4x4 slice. The times are simulated.
128 devices in a mesh: row: 8 (over x, y_hi), col: 16 (over y_lo, z, core).
Axes of the slice: x: 4, y: 4 (y_hi: 2, y_lo: 2; y = y_hi * 2 + y_lo), z: 4, core: 2. Of those that a mesh axis runs over, the one named last changes fastest.
Arguments:
- flat_gradient: bfloat16 [8, 16, 524288], P('row', 'col'), may hold values from -6 to 6
- range_rows: int32 [8, 16], replicated, may hold values from 1 to 64, 512 in all within a row
- left_stat: float32 [4096, 4096], P('row', 'col'), may hold values from -6 to 6
- right_stat: float32 [8192, 8192], P('col', 'row'), may hold values from -6 to 6
- left_root: bfloat16 [4096, 4096], P('row'), as said below
- right_root: bfloat16 [8192, 8192], P('col'), as said below
Outputs:
- left_new: float32 [4096, 4096], P('row', 'col')
- right_new: float32 [8192, 8192], P('col', 'row')
- update: bfloat16 [4096, 8192], P('row', 'col')
Inputs may be any that keep to these rules, and one draw needn't show every extreme that they name: In each row r the entries sum to 512; the largest entry of every row is exactly 64. Slots of flat_gradient beyond a device's range_rows rows are padding. left_root equals its transpose. right_root equals its transpose.
All inputs are finite; a program needn't handle non-finite values.
Results may differ from a plain program's by a relative error of at most 0.014.
Values may be sent and summed in bfloat16 or wider, within the bound.
No kernel may reach another device: no remote copies, remote signals or barrier semaphores. Data moves between devices by JAX's collectives and lax.ppermute only.
A program may use at most 192 MiB of HBM per device.

v0:
```python
import math
import jax
import jax.numpy as jnp
from jax import lax
from jax.sharding import Mesh
from jax.sharding import PartitionSpec as P

HQ = 4096
DIN = 8192
stat_decay = 0.9
COL = ("chip", "core")
ROW = ("x", "yh")


def slot_index(row_counts, tile_rows, capacity):
    offsets = jnp.cumsum(row_counts) - row_counts
    target = jnp.arange(tile_rows, dtype=jnp.int32)
    covered = target[:, None] >= offsets[None, :]
    source = jnp.sum(covered.astype(jnp.int32), axis=1) - 1
    begins = jnp.max(jnp.where(covered, offsets[None, :], 0), axis=1)
    return source * capacity + target - begins


def partner(block):
    return lax.ppermute(block, "core", [(0, 1), (1, 0)])


def shards(flat_gradient, range_rows, left_stat, right_stat, left_root, right_root):
    x_count = lax.axis_size("x")
    row_count = x_count * 2
    chip_count = lax.axis_size("chip")
    col_count = chip_count * 2
    row_index = lax.axis_index(ROW)
    x_index = lax.axis_index("x")
    y_half = lax.axis_index("yh")
    core = lax.axis_index("core")
    tile_rows = HQ // row_count
    tile_cols = DIN // col_count
    slice_rows = tile_rows // col_count
    block_cols = DIN // row_count
    chunk = HQ // col_count
    capacity = flat_gradient.shape[2] // DIN
    held_rows = flat_gradient.reshape(capacity, DIN)
    received = lax.all_to_all(held_rows, COL, split_axis=1, concat_axis=0, tiled=True)
    row_counts = lax.dynamic_index_in_dim(range_rows, row_index, 0, keepdims=False)
    grad_tile = jnp.take(received, slot_index(row_counts, tile_rows, capacity), axis=0)
    row_slice = lax.all_to_all(grad_tile, COL, split_axis=0, concat_axis=1, tiled=True)
    block_piece = lax.all_to_all(row_slice, ROW, split_axis=1, concat_axis=0, tiled=True)
    other_half = lax.ppermute(grad_tile, "yh", [(0, 1), (1, 0)])
    other_half, block_piece = lax.optimization_barrier((other_half, block_piece))
    first = jnp.where(y_half == 0, grad_tile, other_half)
    second = jnp.where(y_half == 0, other_half, grad_tile)
    pair = jnp.stack([first, second])
    moved = [
        lax.ppermute(pair, "x", [(i, (i + s) % x_count) for i in range(x_count)])
        for s in range(1, x_count)
    ]
    row_block = lax.all_gather(block_piece, COL, axis=0, tiled=True)
    panel_parts = jnp.zeros((row_count, tile_rows, tile_cols), grad_tile.dtype)
    panel_parts = lax.dynamic_update_slice_in_dim(panel_parts, pair, 2 * x_index, 0)
    for s in range(1, x_count):
        panel_parts = lax.dynamic_update_slice_in_dim(
            panel_parts, moved[s - 1], 2 * ((x_index - s) % x_count), 0
        )
    column_panel = panel_parts.reshape(HQ, tile_cols)
    left_mixed = jnp.dot(left_root, column_panel, preferred_element_type=jnp.float32).astype(
        jnp.bfloat16
    )
    column_panel, left_mixed, row_block = lax.optimization_barrier(
        (column_panel, left_mixed, row_block)
    )
    col_index = lax.axis_index(COL)
    sub = jnp.arange(chunk, dtype=jnp.int32)
    sub_index = (
        (col_index % 2 * (col_count // 2) + sub // slice_rows) * (row_count * slice_rows)
        + col_index // 2 * slice_rows
        + sub % slice_rows
    )
    sub_rows = jnp.take(row_block, sub_index, axis=0)
    left_part = lax.dot_general(
        row_block, sub_rows, (((1,), (1,)), ((), ())), preferred_element_type=jnp.float32
    )
    left_part = left_part.reshape(col_count, row_count, slice_rows, chunk).transpose(1, 0, 2, 3)
    left_part = left_part.reshape(row_count, tile_rows, chunk)
    pair_parts = left_part.reshape(x_count, 2, tile_rows, chunk)
    outgoing = pair_parts.astype(jnp.bfloat16)
    incoming = [
        lax.ppermute(
            lax.dynamic_index_in_dim(outgoing, (x_index + s) % x_count, 0, keepdims=False),
            "x",
            [(i, (i + s) % x_count) for i in range(x_count)],
        )
        for s in range(1, x_count)
    ]
    panel_reordered = (
        column_panel.reshape(row_count, col_count, slice_rows, tile_cols)
        .transpose(1, 0, 2, 3)
        .reshape(HQ, tile_cols)
    )
    right_gram = lax.dot_general(
        panel_reordered, row_block, (((0,), (0,)), ((), ())), preferred_element_type=jnp.float32
    )
    right_new = stat_decay * right_stat + right_gram * (1.0 / math.sqrt(HQ))
    mixed_rows = lax.all_gather(left_mixed, COL, axis=1, tiled=True)
    incoming, mixed_rows = lax.optimization_barrier((incoming, mixed_rows))
    x_sum = lax.dynamic_index_in_dim(pair_parts, x_index, 0, keepdims=False)
    for part in incoming:
        x_sum = x_sum + part.astype(jnp.float32)
    across = lax.ppermute(
        lax.dynamic_index_in_dim(x_sum, 1 - y_half, 0, keepdims=False).astype(jnp.bfloat16),
        "yh",
        [(0, 1), (1, 0)],
    )
    left_sum = lax.dynamic_index_in_dim(x_sum, y_half, 0, keepdims=False) + across.astype(
        jnp.float32
    )
    update_sum = lax.dot_general(
        mixed_rows, right_root, (((1,), (1,)), ((), ())), preferred_element_type=jnp.float32
    )
    left_new = stat_decay * left_stat + left_sum * (1.0 / math.sqrt(DIN))
    return (left_new, right_new, update_sum.astype(jnp.bfloat16))


def solution(mesh):
    rows, cols = mesh.devices.shape
    split_mesh = Mesh(mesh.devices.reshape(rows // 2, 2, cols // 2, 2), ("x", "yh", "chip", "core"))
    in_specs = (P(ROW, COL, None), P(), P(ROW, COL), P(COL, ROW), P(ROW, None), P(COL, None))
    out_specs = (P(ROW, COL), P(COL, ROW), P(ROW, COL))
    return jax.shard_map(
        shards, mesh=split_mesh, in_specs=in_specs, out_specs=out_specs, check_vma=False
    )
```

profile of v0, /device:TPU:1, one launch (start us, length us, event | category | flops | bytes accessed | tf_op | source)
XLA Modules:
  0.0 226.9 jit_solution(9901679162960642926)
XLA Ops:
  7.2 22.8 %reduce = bf16[524288]{0:T(1024)(128)(2,1)S(1)} reduce(bf16[1,1,524288]{2,1,0:T(2,128)(2,1)} %param.6, bf16[]{:T(256)} %constant.189), dimensions={0,1}, to_apply=%param.6.reduce_sub_computation | reduce | bytes 2097154 | tf_op args[0]
  32.2 7.8 %all-to-all-start = ((bf16[64,16,512]{2,0,1:T(8,128)(2,1)}), bf16[64,16,512]{2,0,1:T(8,128)(2,1)S(1)}, u32[]{:S(2)}, u32[]{:S(2)}) async-start(bf16[64,16,512]{2,0,1:T(8,128)(2,1)} %copy.25), calls=%async_computation | async-start | bytes 2097152 | tf_op jit(solution)/shard_map/all_to_all | solution.py:44
  41.9 13.9 %all-to-all-done = bf16[64,16,512]{2,0,1:T(8,128)(2,1)S(1)} async-done(((bf16[64,16,512]{2,0,1:T(8,128)(2,1)}), bf16[64,16,512]{2,0,1:T(8,128)(2,1)S(1)}, u32[]{:S(2)}, u32[]{:S(2)}) %all-to-all-start) | async-done | bytes 1048608 | tf_op jit(solution)/shard_map/all_to_all | solution.py:44
  55.9 2.0 gather_fusion
  58.8 4.2 %all-to-all-start.1 = ((bf16[16,32,512]{2,1,0:T(8,128)(2,1)}), bf16[16,32,512]{2,1,0:T(8,128)(2,1)S(1)}, u32[]{:S(2)}, u32[]{:S(2)}) async-start(bf16[16,32,512]{2,1,0:T(8,128)(2,1)} %broadcast_select_fusion.1), calls=%async_computation.1 | async-start | bytes 1048576 | tf_op jit(solution)/shard_map/all_to_all | solution.py:47
  63.2 2.7 %collective-permute-start = (bf16[512,512]{1,0:T(8,128)(2,1)S(1)}, bf16[512,512]{1,0:T(8,128)(2,1)S(1)}, u32[]{:S(2)}, u32[]{:S(2)}) collective-permute-start(bf16[512,512]{1,0:T(8,128)(2,1)S(1)} %broadcast_select_fusion), channel_id=1, source_target_pairs={{0,16},{16,0},{1,17},{17,1},{2,18},{18,2},{3,19},{19,3},{4,20},{20... | collective-permute-start | bytes 1572872 | tf_op jit(solution)/shard_map/ppermute | solution.py:49
  65.9 7.3 %all-to-all-done.1 = bf16[16,32,512]{2,1,0:T(8,128)(2,1)S(1)} async-done(((bf16[16,32,512]{2,1,0:T(8,128)(2,1)}), bf16[16,32,512]{2,1,0:T(8,128)(2,1)S(1)}, u32[]{:S(2)}, u32[]{:S(2)}) %all-to-all-start.1) | async-done | bytes 524320 | tf_op jit(solution)/shard_map/all_to_all | solution.py:47
  74.7 6.1 %all-to-all-start.2 = ((bf16[32,8,1024]{2,0,1:T(8,128)(2,1)}), bf16[32,8,1024]{2,0,1:T(8,128)(2,1)S(1)}, u32[]{:S(2)}, u32[]{:S(2)}) async-start(bf16[32,8,1024]{2,0,1:T(8,128)(2,1)} %copy.27), calls=%async_computation.2 | async-start | bytes 1048576 | tf_op jit(solution)/shard_map/all_to_all | solution.py:48
  80.8 2.8 %collective-permute-done = bf16[512,512]{1,0:T(8,128)(2,1)S(1)} collective-permute-done((bf16[512,512]{1,0:T(8,128)(2,1)S(1)}, bf16[512,512]{1,0:T(8,128)(2,1)S(1)}, u32[]{:S(2)}, u32[]{:S(2)}) %collective-permute-start) | collective-permute-done | bytes 524320 | tf_op jit(solution)/shard_map/ppermute | solution.py:49
  83.6 5.8 %all-to-all-done.2 = bf16[32,8,1024]{2,0,1:T(8,128)(2,1)S(1)} async-done(((bf16[32,8,1024]{2,0,1:T(8,128)(2,1)}), bf16[32,8,1024]{2,0,1:T(8,128)(2,1)S(1)}, u32[]{:S(2)}, u32[]{:S(2)}) %all-to-all-start.2) | async-done | bytes 524320 | tf_op jit(solution)/shard_map/all_to_all | solution.py:48
  90.5 2.3 %broadcast_in_dim.40 = bf16[8,512,512]{2,1,0:T(8,128)(2,1)} broadcast(bf16[]{:T(256)} %constant.160.clone.1), dimensions={} | broadcast | bytes 4194306 | tf_op jit(solution)/shard_map/broadcast_in_dim | solution.py:59
  97.5 20.3 %collective-permute-done.1 = bf16[2,512,512]{2,1,0:T(8,128)(2,1)S(1)} collective-permute-done((bf16[2,512,512]{2,1,0:T(8,128)(2,1)}, bf16[2,512,512]{2,1,0:T(8,128)(2,1)S(1)}, u32[]{:S(2)}, u32[]{:S(2)}) %collective-permute-start.1) | collective-permute-done | bytes 1048608 | tf_op jit(solution)/shard_map/ppermute | solution.py:55
  118.9 19.5 %collective-permute-done.2 = bf16[2,512,512]{2,1,0:T(8,128)(2,1)S(1)} collective-permute-done((bf16[2,512,512]{2,1,0:T(8,128)(2,1)}, bf16[2,512,512]{2,1,0:T(8,128)(2,1)S(1)}, u32[]{:S(2)}, u32[]{:S(2)}) %collective-permute-start.2) | collective-permute-done | bytes 1048608 | tf_op jit(solution)/shard_map/ppermute | solution.py:55
  139.4 3.5 %collective-permute-done.3 = bf16[2,512,512]{2,1,0:T(8,128)(2,1)S(1)} collective-permute-done((bf16[2,512,512]{2,1,0:T(8,128)(2,1)}, bf16[2,512,512]{2,1,0:T(8,128)(2,1)S(1)}, u32[]{:S(2)}, u32[]{:S(2)}) %collective-permute-start.3) | collective-permute-done | bytes 1048608 | tf_op jit(solution)/shard_map/ppermute | solution.py:55
  144.0 5.4 %fusion = bf16[512,512]{0,1:T(8,128)(2,1)} fusion(bf16[4096,512]{1,0:T(8,128)(2,1)} %bitcast.12, bf16[512,4096]{1,0:T(8,128)(2,1)S(1)} %copy-done.4), kind=kOutput, calls=%fused_computation.5 | convolution fusion | flops 2147745792 | bytes 8912896 | tf_op jit(solution)/shard_map/dot_general | solution.py:66
  149.6 4.8 %copy.29 = bf16[16,8,32,512]{3,2,1,0:T(8,128)(2,1)} copy(bf16[16,8,32,512]{3,2,0,1:T(8,128)(2,1)} %bitcast.26) | data formatting | bytes 8388608 | tf_op jit(solution)/shard_map/transpose | solution.py:97
  154.3 6.0 %gather_fusion.1 = bf16[256,1024]{1,0:T(8,128)(2,1)S(1)} fusion(bf16[4096,1024]{1,0:T(8,128)(2,1)} %all-gather.3.cloned.1.call-done, s32[1024]{0:T(1024)S(1)} %pad_clamp_fusion), kind=kCustom, calls=%fused_computation.1 | custom fusion | bytes 1049600 | tf_op jit(solution)/shard_map/jit(_take)/gather | solution.py:79
  160.3 5.9 %fusion.5 = f32[4096,256]{1,0:T(8,128)S(1)} fusion(bf16[4096,1024]{1,0:T(8,128)(2,1)} %all-gather.3.cloned.1.call-done, bf16[256,1024]{1,0:T(8,128)(2,1)S(1)} %gather_fusion.1, pred[256]{0:T(512)(128)(4,1)S(1)} %compare_and_fusion.1), kind=kOutput, calls=%fused_computation.17 | convolution fusion | flops 2147745792 | bytes 13107456 | tf_op jit(solution)/shard_map/dot_general | solution.py:80
  170.2 3.0 %collective-permute-start.5 = (bf16[2,512,256]{2,1,0:T(8,128)(2,1)S(1)}, bf16[2,512,256]{2,1,0:T(8,128)(2,1)S(1)}, u32[]{:S(2)}, u32[]{:S(2)}) collective-permute-start(bf16[2,512,256]{2,1,0:T(8,128)(2,1)S(1)} %get-tuple-element.24), channel_id=1, source_target_pairs={{0,64},{32,96},{64,0},{96,32},{1,65},{33,97},{65,1},{97,33},{2,66}... | collective-permute-start | bytes 1572872 | tf_op jit(solution)/shard_map/ppermute | solution.py:88
  173.1 9.5 %multiply_add_fusion = f32[512,1024]{1,0:T(8,128)} fusion(f32[512,1024]{1,0:T(8,128)S(1)} %copy-done.5, bf16[4096,512]{1,0:T(8,128)(2,1)S(1)} %bitcast.60, bf16[4096,1024]{1,0:T(8,128)(2,1)} %all-gather.3.cloned.1.call-done), kind=kOutput, calls=%fused_computation.2 | convolution fusion | flops 4296540160 | bytes 16777216 | tf_op jit(solution)/shard_map/dot_general | solution.py:100
  182.6 13.3 %collective-permute-done.5 = bf16[2,512,256]{2,1,0:T(8,128)(2,1)S(1)} collective-permute-done((bf16[2,512,256]{2,1,0:T(8,128)(2,1)S(1)}, bf16[2,512,256]{2,1,0:T(8,128)(2,1)S(1)}, u32[]{:S(2)}, u32[]{:S(2)}) %collective-permute-start.5) | collective-permute-done | bytes 524320 | tf_op jit(solution)/shard_map/ppermute | solution.py:88
  195.9 7.9 %all-gather.5.cloned.1.call-done = bf16[512,8192]{0,1:T(8,128)(2,1)} async-done(((bf16[512,512]{0,1:T(8,128)(2,1)}), bf16[512,8192]{0,1:T(8,128)(2,1)}) %all-gather.5.cloned.1.call-update) | async-done | bytes 8388624 | tf_op jit(solution)/shard_map/all_gather | solution.py:104
  205.3 2.8 %collective-permute-start.7 = (bf16[512,256]{1,0:T(8,128)(2,1)S(1)}, bf16[512,256]{1,0:T(8,128)(2,1)S(1)}, u32[]{:S(2)}, u32[]{:S(2)}) collective-permute-start(bf16[512,256]{1,0:T(8,128)(2,1)S(1)} %fusion.8), channel_id=1, source_target_pairs={{0,16},{16,0},{1,17},{17,1},{2,18},{18,2},{3,19},{19,3},{4,20},{20... | collective-permute-start | bytes 786440 | tf_op jit(solution)/shard_map/ppermute | solution.py:109
  208.1 11.1 %convolution_convert_fusion = bf16[512,512]{1,0:T(8,128)(2,1)} fusion(bf16[512,8192]{0,1:T(8,128)(2,1)} %all-gather.5.cloned.1.call-done, bf16[512,8192]{1,0:T(8,128)(2,1)} %param.11), kind=kOutput, calls=%fused_computation.3 | convolution fusion | flops 4295229440 | bytes 17301504 | tf_op jit(solution)/shard_map/dot_general | solution.py:117
  (57 shorter events, 22.0 us)
Async XLA Ops:
  32.2 23.7 %all-to-all-start = ((bf16[64,16,512]{2,0,1:T(8,128)(2,1)}), bf16[64,16,512]{2,0,1:T(8,128)(2,1)S(1)}, u32[]{:S(2)}, u32[]{:S(2)}) async-start(bf16[64,16,512]{2,0,1:T(8,128)(2,1)} %copy.25), calls=%async_computation | async-start | bytes 2097152 | tf_op jit(solution)/shard_map/all_to_all | solution.py:44
  58.8 14.4 %all-to-all-start.1 = ((bf16[16,32,512]{2,1,0:T(8,128)(2,1)}), bf16[16,32,512]{2,1,0:T(8,128)(2,1)S(1)}, u32[]{:S(2)}, u32[]{:S(2)}) async-start(bf16[16,32,512]{2,1,0:T(8,128)(2,1)} %broadcast_select_fusion.1), calls=%async_computation.1 | async-start | bytes 1048576 | tf_op jit(solution)/shard_map/all_to_all | solution.py:47
  63.2 20.5 %collective-permute-start = (bf16[512,512]{1,0:T(8,128)(2,1)S(1)}, bf16[512,512]{1,0:T(8,128)(2,1)S(1)}, u32[]{:S(2)}, u32[]{:S(2)}) collective-permute-start(bf16[512,512]{1,0:T(8,128)(2,1)S(1)} %broadcast_select_fusion), channel_id=1, source_target_pairs={{0,16},{16,0},{1,17},{17,1},{2,18},{18,2},{3,19},{19,3},{4,20},{20... | collective-permute-start | bytes 1572872 | tf_op jit(solution)/shard_map/ppermute | solution.py:49
  74.7 14.7 %all-to-all-start.2 = ((bf16[32,8,1024]{2,0,1:T(8,128)(2,1)}), bf16[32,8,1024]{2,0,1:T(8,128)(2,1)S(1)}, u32[]{:S(2)}, u32[]{:S(2)}) async-start(bf16[32,8,1024]{2,0,1:T(8,128)(2,1)} %copy.27), calls=%async_computation.2 | async-start | bytes 1048576 | tf_op jit(solution)/shard_map/all_to_all | solution.py:48
  80.8 68.6 %all-gather.3.cloned.1.call-start = ((), (), s32[]{:S(2)}) async-start(), calls=%async_computation.3 | async-start | bytes 8912896 | tf_op jit(solution)/shard_map/all_gather | solution.py:58
  89.4 0.8 copy-start.2
  90.2 113.6 %all-gather.5.cloned.1.call-start = ((), (), s32[]{:S(2)}) async-start(), calls=%async_computation.4 | async-start | bytes 8912896 | tf_op jit(solution)/shard_map/all_gather | solution.py:104
  94.3 23.6 %collective-permute-start.1 = (bf16[2,512,512]{2,1,0:T(8,128)(2,1)}, bf16[2,512,512]{2,1,0:T(8,128)(2,1)S(1)}, u32[]{:S(2)}, u32[]{:S(2)}) collective-permute-start(bf16[2,512,512]{2,1,0:T(8,128)(2,1)} %get-tuple-element.26), channel_id=1, source_target_pairs={{0,32},{32,64},{64,96},{96,0},{1,33},{33,65},{65,97},{97,1},{2,34}... | collective-permute-start | bytes 3145736 | tf_op jit(solution)/shard_map/ppermute | solution.py:55
  94.6 43.8 %collective-permute-start.2 = (bf16[2,512,512]{2,1,0:T(8,128)(2,1)}, bf16[2,512,512]{2,1,0:T(8,128)(2,1)S(1)}, u32[]{:S(2)}, u32[]{:S(2)}) collective-permute-start(bf16[2,512,512]{2,1,0:T(8,128)(2,1)} %get-tuple-element.26), channel_id=1, source_target_pairs={{0,64},{32,96},{64,0},{96,32},{1,65},{33,97},{65,1},{97,33},{2,66}... | collective-permute-start | bytes 3145736 | tf_op jit(solution)/shard_map/ppermute | solution.py:55
  96.2 46.7 %collective-permute-start.3 = (bf16[2,512,512]{2,1,0:T(8,128)(2,1)}, bf16[2,512,512]{2,1,0:T(8,128)(2,1)S(1)}, u32[]{:S(2)}, u32[]{:S(2)}) collective-permute-start(bf16[2,512,512]{2,1,0:T(8,128)(2,1)} %get-tuple-element.26), channel_id=1, source_target_pairs={{0,96},{32,0},{64,32},{96,64},{1,97},{33,1},{65,33},{97,65},{2,98}... | collective-permute-start | bytes 3145736 | tf_op jit(solution)/shard_map/ppermute | solution.py:55
  97.5 46.5 %copy-start.4 = (bf16[512,4096]{1,0:T(8,128)(2,1)S(1)}, bf16[512,4096]{1,0:T(8,128)(2,1)}, u32[]{:S(2)}) copy-start(bf16[512,4096]{1,0:T(8,128)(2,1)} %param.10) | copy-start | bytes 12582916
  166.6 2.2 copy-start
  166.6 6.5 %copy-start.1 = (bf16[16,8,32,512]{3,2,1,0:T(8,128)(2,1)S(1)}, bf16[16,8,32,512]{3,2,1,0:T(8,128)(2,1)}, u32[]{:S(2)}) copy-start(bf16[16,8,32,512]{3,2,1,0:T(8,128)(2,1)} %copy.29) | copy-start | bytes 12582916
  166.6 6.5 %copy-start.5 = (f32[512,1024]{1,0:T(8,128)S(1)}, f32[512,1024]{1,0:T(8,128)}, u32[]{:S(2)}) copy-start(f32[512,1024]{1,0:T(8,128)} %param.9) | copy-start | bytes 6291460
  168.7 13.9 %collective-permute-start.4 = (bf16[2,512,256]{2,1,0:T(8,128)(2,1)S(1)}, bf16[2,512,256]{2,1,0:T(8,128)(2,1)S(1)}, u32[]{:S(2)}, u32[]{:S(2)}) collective-permute-start(bf16[2,512,256]{2,1,0:T(8,128)(2,1)S(1)} %get-tuple-element.25), channel_id=1, source_target_pairs={{0,32},{32,64},{64,96},{96,0},{1,33},{33,65},{65,97},{97,1},{2,34}... | collective-permute-start | bytes 1572872 | tf_op jit(solution)/shard_map/ppermute | solution.py:88
  170.2 25.7 %collective-permute-start.5 = (bf16[2,512,256]{2,1,0:T(8,128)(2,1)S(1)}, bf16[2,512,256]{2,1,0:T(8,128)(2,1)S(1)}, u32[]{:S(2)}, u32[]{:S(2)}) collective-permute-start(bf16[2,512,256]{2,1,0:T(8,128)(2,1)S(1)} %get-tuple-element.24), channel_id=1, source_target_pairs={{0,64},{32,96},{64,0},{96,32},{1,65},{33,97},{65,1},{97,33},{2,66}... | collective-permute-start | bytes 1572872 | tf_op jit(solution)/shard_map/ppermute | solution.py:88
  173.1 22.8 %collective-permute-start.6 = (bf16[2,512,256]{2,1,0:T(8,128)(2,1)S(1)}, bf16[2,512,256]{2,1,0:T(8,128)(2,1)S(1)}, u32[]{:S(2)}, u32[]{:S(2)}) collective-permute-start(bf16[2,512,256]{2,1,0:T(8,128)(2,1)S(1)} %get-tuple-element.23), channel_id=1, source_target_pairs={{0,96},{32,0},{64,32},{96,64},{1,97},{33,1},{65,33},{97,65},{2,98}... | collective-permute-start | bytes 1572872 | tf_op jit(solution)/shard_map/ppermute | solution.py:88
  205.3 13.9 %copy-start.3 = (f32[512,256]{1,0:T(8,128)S(1)}, f32[512,256]{1,0:T(8,128)}, u32[]{:S(2)}) copy-start(f32[512,256]{1,0:T(8,128)} %param.8) | copy-start | bytes 1572868
  205.3 13.9 %collective-permute-start.7 = (bf16[512,256]{1,0:T(8,128)(2,1)S(1)}, bf16[512,256]{1,0:T(8,128)(2,1)S(1)}, u32[]{:S(2)}, u32[]{:S(2)}) collective-permute-start(bf16[512,256]{1,0:T(8,128)(2,1)S(1)} %fusion.8), channel_id=1, source_target_pairs={{0,16},{16,0},{1,17},{17,1},{2,18},{18,2},{3,19},{19,3},{4,20},{20... | collective-permute-start | bytes 786440 | tf_op jit(solution)/shard_map/ppermute | solution.py:109
Sparse Core Ops, SparseCore 0:
  90.4 52.3 all-gather.2
  149.6 54.1 all-gather.4
where the time goes:
time: 228 us; the launch traced here: 227 us
  waiting for transfers between devices  94.4 us (41%)
  matrix products  31.9 us (14%)
  starting transfers between devices  31.4 us (14%)
  other arithmetic  29.1 us (13%)
  local copies, waits for them, and re-layouts  25.9 us (11%)
  between operations  14.3 us (6%)
    ppermute x3, waiting for transfers between devices, shards(): lax.ppermute(pair, 'x', [(i, (i + s) % x_count) for i in range(x_count)])  43.3 us
    unnamed x1, other arithmetic  22.8 us
    all_to_all x1, waiting for transfers between devices, shards(): lax.all_to_all(held_rows, COL, split_axis=1, concat_axis=0, tiled=True)  13.9 us
    ppermute x3, waiting for transfers between devices, shards(): lax.ppermute(lax.dynamic_index_in_dim(outgoing, (x_index + s) % x_count,...  13.3 us
    dot_general x1, matrix products, shards(): lax.dot_general(mixed_rows, right_root, (((1,), (1,)), ((), ())), preferr...  11.1 us
    dot_general x1, matrix products, shards(): lax.dot_general(panel_reordered, row_block, (((0,), (0,)), ((), ())), pre...  9.46 us
    all_gather x1, waiting for transfers between devices, shards(): mixed_rows = lax.all_gather(left_mixed, COL, axis=1, tiled=True)  7.9 us
    all_to_all x1, starting transfers between devices, shards(): lax.all_to_all(held_rows, COL, split_axis=1, concat_axis=0, tiled=True)  7.84 us
  transfers between devices with their start and end apart: 13, of which 9 were waited for; matrix products, arithmetic and copies ran while one was open for 24% of the time, Pallas kernels for 0%

commit v1 on v0

--- a/solution.py
+++ b/solution.py
@@ -101,7 +101,9 @@
         panel_reordered, row_block, (((0,), (0,)), ((), ())), preferred_element_type=jnp.float32
     )
     right_new = stat_decay * right_stat + right_gram * (1.0 / math.sqrt(HQ))
-    mixed_rows = lax.all_gather(left_mixed, COL, axis=1, tiled=True)
+    mixed_rows = jnp.concatenate(
+        lax.all_to_all(jnp.stack([left_mixed] * lax.axis_size(COL)), COL, 0, 0), axis=1
+    )
     incoming, mixed_rows = lax.optimization_barrier((incoming, mixed_rows))
     x_sum = lax.dynamic_index_in_dim(pair_parts, x_index, 0, keepdims=False)
     for part in incoming:

time: 228 us -> 311 us (1.36); the launches traced: 227 us -> 306 us
  waiting for transfers between devices: 94.4 us -> 164 us
  starting transfers between devices: 31.4 us -> 37.2 us
  local copies, waits for them, and re-layouts: 25.9 us -> 29.9 us
    all_to_all x0 -> x1, waiting for transfers between devices: none -> 77 us  [shards(): lax.all_to_all(jnp.stack([left_mixed] * lax.axis_size(COL)), COL, 0, 0)]
    all_to_all x0 -> x1, starting transfers between devices: none -> 8.52 us  [shards(): lax.all_to_all(jnp.stack([left_mixed] * lax.axis_size(COL)), COL, 0, 0)]
    all_gather x1 -> x0, waiting for transfers between devices: 7.9 us -> none  [shards(): mixed_rows = lax.all_gather(left_mixed, COL, axis=1, tiled=True)]
    another operation x0 -> x1, local copies, waits for them, and re-layouts: none -> 4.04 us  [shards(): jnp.stack([left_mixed] * lax.axis_size(COL))]
  transfers between devices with their start and end apart: 13 -> 13, of which waited for: 9 -> 11; matrix products, arithmetic and copies ran while one was open for 24% -> 17% of each run, Pallas kernels for 0% -> 0%
where the time goes in v1:
time: 311 us; the launch traced here: 306 us
  waiting for transfers between devices  164 us (53%)
  starting transfers between devices  37.2 us (12%)
  matrix products  30.9 us (10%)
  local copies, waits for them, and re-layouts  29.9 us (10%)
  other arithmetic  29.2 us (9%)
  between operations  14.2 us (5%)
    all_to_all x1, waiting for transfers between devices, shards(): lax.all_to_all(jnp.stack([left_mixed] * lax.axis_size(COL)), COL, 0, 0)  77 us
    ppermute x3, waiting for transfers between devices, shards(): lax.ppermute(pair, 'x', [(i, (i + s) % x_count) for i in range(x_count)])  43.3 us
    unnamed x1, other arithmetic  22.8 us
    ppermute x3, waiting for transfers between devices, shards(): lax.ppermute(lax.dynamic_index_in_dim(outgoing, (x_index + s) % x_count,...  14.2 us
    all_to_all x1, waiting for transfers between devices, shards(): lax.all_to_all(held_rows, COL, split_axis=1, concat_axis=0, tiled=True)  13.9 us
    dot_general x1, matrix products, shards(): lax.dot_general(mixed_rows, right_root, (((1,), (1,)), ((), ())), preferr...  11.1 us
    dot_general x1, matrix products, shards(): lax.dot_general(panel_reordered, row_block, (((0,), (0,)), ((), ())), pre...  9.3 us
    all_to_all x1, starting transfers between devices, shards(): lax.all_to_all(jnp.stack([left_mixed] * lax.axis_size(COL)), COL, 0, 0)  8.52 us
  transfers between devices with their start and end apart: 13, of which 11 were waited for; matrix products, arithmetic and copies ran while one was open for 17% of the time, Pallas kernels for 0%

profile of v1, /device:TPU:1, one launch (start us, length us, event | category | flops | bytes accessed | tf_op | source)
XLA Modules:
  0.0 305.7 jit_solution(16287160029643950053)
XLA Ops:
  7.2 22.8 %reduce = bf16[524288]{0:T(1024)(128)(2,1)S(1)} reduce(bf16[1,1,524288]{2,1,0:T(2,128)(2,1)} %param.6, bf16[]{:T(256)} %constant.189), dimensions={0,1}, to_apply=%param.6.reduce_sub_computation | reduce | bytes 2097154 | tf_op args[0]
  32.2 7.8 %all-to-all-start = ((bf16[64,16,512]{2,0,1:T(8,128)(2,1)}), bf16[64,16,512]{2,0,1:T(8,128)(2,1)S(1)}, u32[]{:S(2)}, u32[]{:S(2)}) async-start(bf16[64,16,512]{2,0,1:T(8,128)(2,1)} %copy.26), calls=%async_computation | async-start | bytes 2097152 | tf_op jit(solution)/shard_map/all_to_all | solution.py:44
  41.9 13.9 %all-to-all-done = bf16[64,16,512]{2,0,1:T(8,128)(2,1)S(1)} async-done(((bf16[64,16,512]{2,0,1:T(8,128)(2,1)}), bf16[64,16,512]{2,0,1:T(8,128)(2,1)S(1)}, u32[]{:S(2)}, u32[]{:S(2)}) %all-to-all-start) | async-done | bytes 1048608 | tf_op jit(solution)/shard_map/all_to_all | solution.py:44
  58.8 4.2 %all-to-all-start.1 = ((bf16[16,32,512]{2,1,0:T(8,128)(2,1)}), bf16[16,32,512]{2,1,0:T(8,128)(2,1)S(1)}, u32[]{:S(2)}, u32[]{:S(2)}) async-start(bf16[16,32,512]{2,1,0:T(8,128)(2,1)} %broadcast_select_fusion.1), calls=%async_computation.1 | async-start | bytes 1048576 | tf_op jit(solution)/shard_map/all_to_all | solution.py:47
  63.2 2.7 collective-permute-start
  65.9 7.3 %all-to-all-done.1 = bf16[16,32,512]{2,1,0:T(8,128)(2,1)S(1)} async-done(((bf16[16,32,512]{2,1,0:T(8,128)(2,1)}), bf16[16,32,512]{2,1,0:T(8,128)(2,1)S(1)}, u32[]{:S(2)}, u32[]{:S(2)}) %all-to-all-start.1) | async-done | bytes 524320 | tf_op jit(solution)/shard_map/all_to_all | solution.py:47
  74.7 6.1 %all-to-all-start.2 = ((bf16[32,8,1024]{2,0,1:T(8,128)(2,1)}), bf16[32,8,1024]{2,0,1:T(8,128)(2,1)S(1)}, u32[]{:S(2)}, u32[]{:S(2)}) async-start(bf16[32,8,1024]{2,0,1:T(8,128)(2,1)} %copy.28), calls=%async_computation.2 | async-start | bytes 1048576 | tf_op jit(solution)/shard_map/all_to_all | solution.py:48
  80.8 2.8 collective-permute-done
  83.6 5.8 %all-to-all-done.2 = bf16[32,8,1024]{2,0,1:T(8,128)(2,1)S(1)} async-done(((bf16[32,8,1024]{2,0,1:T(8,128)(2,1)}), bf16[32,8,1024]{2,0,1:T(8,128)(2,1)S(1)}, u32[]{:S(2)}, u32[]{:S(2)}) %all-to-all-start.2) | async-done | bytes 524320 | tf_op jit(solution)/shard_map/all_to_all | solution.py:48
  90.4 2.3 broadcast_in_dim.40
  97.5 20.4 %collective-permute-done.1 = bf16[2,512,512]{2,1,0:T(8,128)(2,1)S(1)} collective-permute-done((bf16[2,512,512]{2,1,0:T(8,128)(2,1)}, bf16[2,512,512]{2,1,0:T(8,128)(2,1)S(1)}, u32[]{:S(2)}, u32[]{:S(2)}) %collective-permute-start.1) | collective-permute-done | bytes 1048608 | tf_op jit(solution)/shard_map/ppermute | solution.py:55
  119.0 19.4 %collective-permute-done.2 = bf16[2,512,512]{2,1,0:T(8,128)(2,1)S(1)} collective-permute-done((bf16[2,512,512]{2,1,0:T(8,128)(2,1)}, bf16[2,512,512]{2,1,0:T(8,128)(2,1)S(1)}, u32[]{:S(2)}, u32[]{:S(2)}) %collective-permute-start.2) | collective-permute-done | bytes 1048608 | tf_op jit(solution)/shard_map/ppermute | solution.py:55
  139.4 3.5 %collective-permute-done.3 = bf16[2,512,512]{2,1,0:T(8,128)(2,1)S(1)} collective-permute-done((bf16[2,512,512]{2,1,0:T(8,128)(2,1)}, bf16[2,512,512]{2,1,0:T(8,128)(2,1)S(1)}, u32[]{:S(2)}, u32[]{:S(2)}) %collective-permute-start.3) | collective-permute-done | bytes 1048608 | tf_op jit(solution)/shard_map/ppermute | solution.py:55
  144.0 4.6 %fusion = bf16[512,512]{0,1:T(8,128)(2,1)S(1)} fusion(bf16[4096,512]{1,0:T(8,128)(2,1)} %bitcast.12, bf16[512,4096]{1,0:T(8,128)(2,1)S(1)} %copy-done.4), kind=kOutput, calls=%fused_computation.5 | convolution fusion | flops 2147745792 | bytes 8912896 | tf_op jit(solution)/shard_map/dot_general | solution.py:66
  148.7 4.0 %stack.11 = bf16[16,512,512]{1,2,0:T(8,128)(2,1)} broadcast(bf16[512,512]{0,1:T(8,128)(2,1)S(1)} %fusion), dimensions={1,2} | broadcast | bytes 8912896 | tf_op jit(solution)/shard_map/stack | solution.py:105
  152.7 8.5 %all-to-all-start.3 = ((bf16[16,512,512]{1,2,0:T(8,128)(2,1)}), bf16[16,512,512]{1,2,0:T(8,128)(2,1)}, u32[]{:S(2)}, u32[]{:S(2)}) async-start(bf16[16,512,512]{1,2,0:T(8,128)(2,1)} %stack.11), calls=%async_computation.3 | async-start | bytes 16777216 | tf_op jit(solution)/shard_map/all_to_all | solution.py:105
  161.3 4.7 %copy.30 = bf16[16,8,32,512]{3,2,1,0:T(8,128)(2,1)} copy(bf16[16,8,32,512]{3,2,0,1:T(8,128)(2,1)} %bitcast.28) | data formatting | bytes 8388608 | tf_op jit(solution)/shard_map/transpose | solution.py:97
  166.0 6.0 %gather_fusion.1 = bf16[256,1024]{1,0:T(8,128)(2,1)S(1)} fusion(bf16[4096,1024]{1,0:T(8,128)(2,1)} %all-gather.2.cloned.1.call-done, s32[1024]{0:T(1024)S(1)} %pad_clamp_fusion), kind=kCustom, calls=%fused_computation.1 | custom fusion | bytes 1049600 | tf_op jit(solution)/shard_map/jit(_take)/gather | solution.py:79
  172.0 5.8 %fusion.5 = f32[4096,256]{1,0:T(8,128)S(1)} fusion(bf16[4096,1024]{1,0:T(8,128)(2,1)} %all-gather.2.cloned.1.call-done, bf16[256,1024]{1,0:T(8,128)(2,1)S(1)} %gather_fusion.1, pred[256]{0:T(512)(128)(4,1)S(1)} %compare_and_fusion.1), kind=kOutput, calls=%fused_computation.17 | convolution fusion | flops 2147745792 | bytes 13107456 | tf_op jit(solution)/shard_map/dot_general | solution.py:80
  183.0 9.3 %multiply_add_fusion = f32[512,1024]{1,0:T(8,128)} fusion(f32[512,1024]{1,0:T(8,128)S(1)} %copy-done.5, bf16[4096,512]{1,0:T(8,128)(2,1)S(1)} %bitcast.63, bf16[4096,1024]{1,0:T(8,128)(2,1)} %all-gather.2.cloned.1.call-done), kind=kOutput, calls=%fused_computation.2 | convolution fusion | flops 4296540160 | bytes 16777216 | tf_op jit(solution)/shard_map/dot_general | solution.py:100
  192.3 3.2 %collective-permute-done.4 = bf16[2,512,256]{2,1,0:T(8,128)(2,1)S(1)} collective-permute-done((bf16[2,512,256]{2,1,0:T(8,128)(2,1)S(1)}, bf16[2,512,256]{2,1,0:T(8,128)(2,1)S(1)}, u32[]{:S(2)}, u32[]{:S(2)}) %collective-permute-start.4) | collective-permute-done | bytes 524320 | tf_op jit(solution)/shard_map/ppermute | solution.py:88
  195.5 10.1 %collective-permute-done.5 = bf16[2,512,256]{2,1,0:T(8,128)(2,1)S(1)} collective-permute-done((bf16[2,512,256]{2,1,0:T(8,128)(2,1)S(1)}, bf16[2,512,256]{2,1,0:T(8,128)(2,1)S(1)}, u32[]{:S(2)}, u32[]{:S(2)}) %collective-permute-start.5) | collective-permute-done | bytes 524320 | tf_op jit(solution)/shard_map/ppermute | solution.py:88
  206.5 77.0 %all-to-all-done.3 = bf16[16,512,512]{1,2,0:T(8,128)(2,1)} async-done(((bf16[16,512,512]{1,2,0:T(8,128)(2,1)}), bf16[16,512,512]{1,2,0:T(8,128)(2,1)}, u32[]{:S(2)}, u32[]{:S(2)}) %all-to-all-start.3) | async-done | bytes 8388640 | tf_op jit(solution)/shard_map/all_to_all | solution.py:105
  286.9 11.1 %convolution_convert_fusion = bf16[512,512]{1,0:T(8,128)(2,1)} fusion(bf16[512,8192]{0,1:T(8,128)(2,1)} %bitcast.24, bf16[512,8192]{1,0:T(8,128)(2,1)} %param.11), kind=kOutput, calls=%fused_computation.3 | convolution fusion | flops 4295229440 | bytes 17301504 | tf_op jit(solution)/shard_map/dot_general | solution.py:119
  (57 shorter events, 27.9 us)
Async XLA Ops:
  32.2 23.7 %all-to-all-start = ((bf16[64,16,512]{2,0,1:T(8,128)(2,1)}), bf16[64,16,512]{2,0,1:T(8,128)(2,1)S(1)}, u32[]{:S(2)}, u32[]{:S(2)}) async-start(bf16[64,16,512]{2,0,1:T(8,128)(2,1)} %copy.26), calls=%async_computation | async-start | bytes 2097152 | tf_op jit(solution)/shard_map/all_to_all | solution.py:44
  58.8 14.4 %all-to-all-start.1 = ((bf16[16,32,512]{2,1,0:T(8,128)(2,1)}), bf16[16,32,512]{2,1,0:T(8,128)(2,1)S(1)}, u32[]{:S(2)}, u32[]{:S(2)}) async-start(bf16[16,32,512]{2,1,0:T(8,128)(2,1)} %broadcast_select_fusion.1), calls=%async_computation.1 | async-start | bytes 1048576 | tf_op jit(solution)/shard_map/all_to_all | solution.py:47
  63.2 20.5 %collective-permute-start = (bf16[512,512]{1,0:T(8,128)(2,1)S(1)}, bf16[512,512]{1,0:T(8,128)(2,1)S(1)}, u32[]{:S(2)}, u32[]{:S(2)}) collective-permute-start(bf16[512,512]{1,0:T(8,128)(2,1)S(1)} %broadcast_select_fusion), channel_id=1, source_target_pairs={{0,16},{16,0},{1,17},{17,1},{2,18},{18,2},{3,19},{19,3},{4,20},{20... | collective-permute-start | bytes 1572872 | tf_op jit(solution)/shard_map/ppermute | solution.py:49
  74.7 14.7 %all-to-all-start.2 = ((bf16[32,8,1024]{2,0,1:T(8,128)(2,1)}), bf16[32,8,1024]{2,0,1:T(8,128)(2,1)S(1)}, u32[]{:S(2)}, u32[]{:S(2)}) async-start(bf16[32,8,1024]{2,0,1:T(8,128)(2,1)} %copy.28), calls=%async_computation.2 | async-start | bytes 1048576 | tf_op jit(solution)/shard_map/all_to_all | solution.py:48
  80.8 67.9 %all-gather.2.cloned.1.call-start = ((), (), s32[]{:S(2)}) async-start(), calls=%async_computation.4 | async-start | bytes 8912896 | tf_op jit(solution)/shard_map/all_gather | solution.py:58
  89.4 0.8 copy-start.2
  94.3 23.6 %collective-permute-start.1 = (bf16[2,512,512]{2,1,0:T(8,128)(2,1)}, bf16[2,512,512]{2,1,0:T(8,128)(2,1)S(1)}, u32[]{:S(2)}, u32[]{:S(2)}) collective-permute-start(bf16[2,512,512]{2,1,0:T(8,128)(2,1)} %get-tuple-element.26), channel_id=1, source_target_pairs={{0,32},{32,64},{64,96},{96,0},{1,33},{33,65},{65,97},{97,1},{2,34}... | collective-permute-start | bytes 3145736 | tf_op jit(solution)/shard_map/ppermute | solution.py:55
  94.5 43.9 %collective-permute-start.2 = (bf16[2,512,512]{2,1,0:T(8,128)(2,1)}, bf16[2,512,512]{2,1,0:T(8,128)(2,1)S(1)}, u32[]{:S(2)}, u32[]{:S(2)}) collective-permute-start(bf16[2,512,512]{2,1,0:T(8,128)(2,1)} %get-tuple-element.26), channel_id=1, source_target_pairs={{0,64},{32,96},{64,0},{96,32},{1,65},{33,97},{65,1},{97,33},{2,66}... | collective-permute-start | bytes 3145736 | tf_op jit(solution)/shard_map/ppermute | solution.py:55
  96.2 46.8 %collective-permute-start.3 = (bf16[2,512,512]{2,1,0:T(8,128)(2,1)}, bf16[2,512,512]{2,1,0:T(8,128)(2,1)S(1)}, u32[]{:S(2)}, u32[]{:S(2)}) collective-permute-start(bf16[2,512,512]{2,1,0:T(8,128)(2,1)} %get-tuple-element.26), channel_id=1, source_target_pairs={{0,96},{32,0},{64,32},{96,64},{1,97},{33,1},{65,33},{97,65},{2,98}... | collective-permute-start | bytes 3145736 | tf_op jit(solution)/shard_map/ppermute | solution.py:55
  97.5 46.5 %copy-start.4 = (bf16[512,4096]{1,0:T(8,128)(2,1)S(1)}, bf16[512,4096]{1,0:T(8,128)(2,1)}, u32[]{:S(2)}) copy-start(bf16[512,4096]{1,0:T(8,128)(2,1)} %param.10) | copy-start | bytes 12582916
  152.7 130.8 %all-to-all-start.3 = ((bf16[16,512,512]{1,2,0:T(8,128)(2,1)}), bf16[16,512,512]{1,2,0:T(8,128)(2,1)}, u32[]{:S(2)}, u32[]{:S(2)}) async-start(bf16[16,512,512]{1,2,0:T(8,128)(2,1)} %stack.11), calls=%async_computation.3 | async-start | bytes 16777216 | tf_op jit(solution)/shard_map/all_to_all | solution.py:105
  178.2 2.1 copy-start
  178.2 4.8 %copy-start.1 = (bf16[16,8,32,512]{3,2,1,0:T(8,128)(2,1)S(1)}, bf16[16,8,32,512]{3,2,1,0:T(8,128)(2,1)}, u32[]{:S(2)}) copy-start(bf16[16,8,32,512]{3,2,1,0:T(8,128)(2,1)} %copy.30) | copy-start | bytes 12582916
  178.2 4.8 %copy-start.5 = (f32[512,1024]{1,0:T(8,128)S(1)}, f32[512,1024]{1,0:T(8,128)}, u32[]{:S(2)}) copy-start(f32[512,1024]{1,0:T(8,128)} %param.9) | copy-start | bytes 6291460
  180.3 15.2 %collective-permute-start.4 = (bf16[2,512,256]{2,1,0:T(8,128)(2,1)S(1)}, bf16[2,512,256]{2,1,0:T(8,128)(2,1)S(1)}, u32[]{:S(2)}, u32[]{:S(2)}) collective-permute-start(bf16[2,512,256]{2,1,0:T(8,128)(2,1)S(1)} %get-tuple-element.25), channel_id=1, source_target_pairs={{0,32},{32,64},{64,96},{96,0},{1,33},{33,65},{65,97},{97,1},{2,34}... | collective-permute-start | bytes 1572872 | tf_op jit(solution)/shard_map/ppermute | solution.py:88
  180.3 25.3 %collective-permute-start.5 = (bf16[2,512,256]{2,1,0:T(8,128)(2,1)S(1)}, bf16[2,512,256]{2,1,0:T(8,128)(2,1)S(1)}, u32[]{:S(2)}, u32[]{:S(2)}) collective-permute-start(bf16[2,512,256]{2,1,0:T(8,128)(2,1)S(1)} %get-tuple-element.24), channel_id=1, source_target_pairs={{0,64},{32,96},{64,0},{96,32},{1,65},{33,97},{65,1},{97,33},{2,66}... | collective-permute-start | bytes 1572872 | tf_op jit(solution)/shard_map/ppermute | solution.py:88
  182.4 24.1 %collective-permute-start.6 = (bf16[2,512,256]{2,1,0:T(8,128)(2,1)S(1)}, bf16[2,512,256]{2,1,0:T(8,128)(2,1)S(1)}, u32[]{:S(2)}, u32[]{:S(2)}) collective-permute-start(bf16[2,512,256]{2,1,0:T(8,128)(2,1)S(1)} %get-tuple-element.23), channel_id=1, source_target_pairs={{0,96},{32,0},{64,32},{96,64},{1,97},{33,1},{65,33},{97,65},{2,98}... | collective-permute-start | bytes 1572872 | tf_op jit(solution)/shard_map/ppermute | solution.py:88
  285.0 13.0 %copy-start.3 = (f32[512,256]{1,0:T(8,128)S(1)}, f32[512,256]{1,0:T(8,128)}, u32[]{:S(2)}) copy-start(f32[512,256]{1,0:T(8,128)} %param.8) | copy-start | bytes 1572868
  285.0 13.0 %collective-permute-start.7 = (bf16[512,256]{1,0:T(8,128)(2,1)S(1)}, bf16[512,256]{1,0:T(8,128)(2,1)S(1)}, u32[]{:S(2)}, u32[]{:S(2)}) collective-permute-start(bf16[512,256]{1,0:T(8,128)(2,1)S(1)} %fusion.8), channel_id=1, source_target_pairs={{0,16},{16,0},{1,17},{17,1},{2,18},{18,2},{3,19},{19,3},{4,20},{20... | collective-permute-start | bytes 786440 | tf_op jit(solution)/shard_map/ppermute | solution.py:111
Sparse Core Ops, SparseCore 0:
  90.4 52.3 all-gather.1
